TPU v7x, 32 devices: a whole 2x2x4 slice. The times are simulated.
32 devices in a mesh: dp: 8 (over y, x, core), tensor: 4 (over z).
Axes of the slice: x: 2, y: 2, z: 4, core: 2. Of those that a mesh axis runs over, the one named last changes fastest.
Arguments:
- acts: bfloat16 [4096, 2048], P('dp', 'tensor'), may hold values from -6 to 6
- out_grads: bfloat16 [4096, 8192], P('dp', 'tensor'), may hold values from -6 to 6
- basis_out: bfloat16 [8192, 8192], P('tensor'), may hold values from -0.0625 to 0.0625
- basis_in: bfloat16 [2048, 2048], P('tensor'), may hold values from -0.125 to 0.125
- slot_sequence: int32 [16], replicated, may hold values from 0 to 15, each once
- seq_lengths: int32 [16], replicated, may hold values from 1 to 256, 2560 in all
Outputs:
- eigenvalues: float32 [8192, 2048], P('tensor', 'dp')
Inputs may be any that keep to these rules, and one draw needn't show every extreme that they name: `slot_sequence`: every sequence number appears exactly once. `seq_lengths`: the largest count is exactly 256.
All inputs are finite; a program needn't handle non-finite values.
Results may differ from a plain program's by a relative error of at most 0.0018.
Values may be sent and summed in bfloat16 or wider, within the bound.
No kernel may reach another device: no remote copies, remote signals or barrier semaphores. Data moves between devices by JAX's collectives and lax.ppermute only.
A program may use at most 128 MiB of HBM per device.

v0:
```python
import jax
import jax.numpy as jnp
from jax import lax
from jax.sharding import PartitionSpec as P

LEN = 256
VALID_NUM, VALID_DEN = (5, 8)
CHUNKS = 4


def redistribute(x, dp):
    slots = x.shape[0] // LEN
    width = x.shape[1]
    x = x.reshape(slots, LEN // dp, dp, width).transpose(2, 0, 1, 3).reshape(-1, width)
    return lax.all_to_all(x, "dp", 0, 0, tiled=True)


def shards(acts, out_grads, basis_out, basis_in, slot_sequence, seq_lengths, *, dp, tp):
    tok_rows = acts.shape[0]
    nseq = seq_lengths.shape[0]
    per = LEN // dp
    total = nseq * LEN * VALID_NUM // VALID_DEN
    cap = -(-(total + nseq * (dp - 1)) // dp)
    cap = -(-cap // 16) * 16
    rows_all = dp * cap
    group = lax.axis_index("dp")
    counts = seq_lengths[slot_sequence]
    groups = jnp.arange(dp, dtype=jnp.int32)
    kept = jnp.clip((counts[:, None] - groups[None, :] + dp - 1) // dp, 0, per)
    ends = jnp.cumsum(kept, axis=0)
    starts = ends - kept
    my_ends = ends[:, group]
    my_starts = starts[:, group]
    rows = jnp.arange(cap, dtype=jnp.int32)
    slot_of = jnp.sum((my_ends[None, :] <= rows[:, None]).astype(jnp.int32), axis=1)
    in_use = slot_of < nseq
    slot_c = jnp.minimum(slot_of, nseq - 1)
    src = jnp.clip(slot_c * per + rows - my_starts[slot_c], 0, nseq * per - 1)
    grads_r = redistribute(out_grads, dp)
    grads_p = jnp.take(grads_r, src, axis=0, mode="clip")
    grads_p = jnp.where(in_use[:, None], grads_p, jnp.zeros_like(grads_p))
    acts_r = redistribute(acts, dp)
    acts_p = jnp.take(acts_r, src, axis=0, mode="clip")
    act_part = jnp.dot(acts_p, basis_in, preferred_element_type=jnp.float32)
    act_sum = lax.psum_scatter(act_part, "tensor", scatter_dimension=1, tiled=True)
    act_whole = lax.all_gather(act_sum.astype(jnp.bfloat16), "tensor", axis=1, tiled=True)
    in_cols = act_whole.shape[1] // dp
    act_whole = act_whole.reshape(cap, dp, in_cols).transpose(1, 0, 2).reshape(-1, in_cols)
    rot_acts = lax.all_to_all(act_whole, "dp", 0, 0, tiled=True)
    lo = groups[None, :] * cap + starts
    win = jnp.minimum(lo, rows_all - per)
    js = jnp.arange(per, dtype=jnp.int32)
    at = win[:, :, None] + js[None, None, :]
    live = (at >= lo[:, :, None]) & (at < (lo + kept)[:, :, None])

    def windows(rows_of, slot):
        return jnp.concatenate(
            [lax.dynamic_slice_in_dim(rows_of, win[slot, g], per, 0) for g in range(dp)]
        )

    units = cap // 16
    bounds = [16 * (c * units // CHUNKS) for c in range(CHUNKS + 1)]
    pieces = []
    for c in range(CHUNKS):
        if c == 1:
            grads_p, rot_acts = lax.optimization_barrier((grads_p, rot_acts))
        block = grads_p[bounds[c] : bounds[c + 1]]
        grad_part = jnp.dot(block, basis_out, preferred_element_type=jnp.float32)
        rot_grads = lax.psum_scatter(grad_part, "tensor", scatter_dimension=1, tiled=True)
        rot_grads = rot_grads.astype(jnp.bfloat16)
        sent = jnp.broadcast_to(rot_grads[None], (dp,) + rot_grads.shape).reshape(
            -1, rot_grads.shape[1]
        )
        got = lax.all_to_all(sent, "dp", 0, 0, tiled=True)
        pieces.append(got.reshape(dp, -1, got.shape[1]))
    all_grads = jnp.concatenate(pieces, axis=1).reshape(rows_all, -1)

    def one_slot(slot, squares):
        g_s = windows(all_grads, slot)
        a_s = windows(rot_acts, slot)
        a_s = jnp.where(live[slot].reshape(-1, 1), a_s, jnp.zeros_like(a_s))
        rotated = lax.dot_general(
            g_s, a_s, (((0,), (0,)), ((), ())), preferred_element_type=jnp.float32
        )
        return squares + rotated * rotated

    squares = jnp.zeros((all_grads.shape[1], rot_acts.shape[1]), jnp.float32)
    squares = lax.fori_loop(0, nseq, one_slot, squares)
    return squares / (nseq * LEN)


def solution(mesh):
    dp = mesh.shape["dp"]
    tp = mesh.shape["tensor"]

    def body(*args):
        return shards(*args, dp=dp, tp=tp)

    return jax.shard_map(
        body,
        mesh=mesh,
        in_specs=(
            P("dp", "tensor"),
            P("dp", "tensor"),
            P("tensor", None),
            P("tensor", None),
            P(),
            P(),
        ),
        out_specs=P("tensor", "dp"),
        check_vma=False,
    )
```

profile of v0, /device:TPU:0, one launch (start us, length us, event | category | flops | bytes accessed | tf_op | source)
XLA Modules:
  0.0 841.4 jit_solution(1465902554699397482)
XLA Ops:
  8.7 5.2 all-to-all-start.2
  17.2 4.3 fusion.22
  21.5 5.7 select_select_fusion
  35.8 4.1 all-to-all-start
  40.0 26.6 %all-to-all-done = bf16[8,64,2048]{2,1,0:T(8,128)(2,1)S(1)} async-done(((bf16[8,64,2048]{2,1,0:T(8,128)(2,1)}), bf16[8,64,2048]{2,1,0:T(8,128)(2,1)S(1)}, u32[]{:S(2)}, u32[]{:S(2)}) %all-to-all-start) | async-done | bytes 2097184 | tf_op jit(solution)/shard_map/all_to_all | solution.py:15
  69.0 18.9 %reduce-scatter.8.cloned.1.call-done = f32[336,512]{1,0:T(8,128)} async-done(((f32[336,2048]{1,0:T(8,128)}), f32[336,512]{1,0:T(8,128)}) %reduce-scatter.8.cloned.1.call-update) | async-done | bytes 688144 | tf_op jit(solution)/shard_map/reduce_scatter | solution.py:45
  90.0 15.4 %fusion.7 = f32[80,8192]{1,0:T(8,128)} fusion(bf16[2048,8192]{1,0:T(8,128)(2,1)} %param.10, bf16[336,2048]{1,0:T(8,128)(2,1)S(1)} %broadcast_select_fusion), kind=kOutput, calls=%fused_computation.40 | convolution fusion | flops 2684354560 | bytes 36503552 | tf_op jit(solution)/shard_map/dot_general | solution.py:68
  105.5 17.7 %all-gather.2.cloned.1.call-done = bf16[336,2048]{1,0:T(8,128)(2,1)} async-done(((bf16[336,512]{1,0:T(8,128)(2,1)}), bf16[336,2048]{1,0:T(8,128)(2,1)}) %all-gather.2.cloned.1.call-update) | async-done | bytes 1376272 | tf_op jit(solution)/shard_map/all_gather | solution.py:46
  124.7 22.3 %all_to_all.57 = bf16[8,336,256]{2,1,0:T(8,128)(2,1)S(1)} all-to-all(bf16[8,336,256]{2,1,0:T(8,128)(2,1)S(1)} %bitcast.72), channel_id=1, replica_groups=mesh['dp'=8,'tensor'=4] {'dp'}, dimensions={0} | all-to-all | bytes 2752512 | tf_op jit(solution)/shard_map/all_to_all | solution.py:49
  147.0 15.2 %fusion.11 = f32[80,8192]{1,0:T(8,128)} fusion(bf16[2048,8192]{1,0:T(8,128)(2,1)} %param.10, bf16[336,2048]{1,0:T(8,128)(2,1)S(1)} %broadcast_select_fusion), kind=kOutput, calls=%fused_computation.44 | convolution fusion | flops 2684354560 | bytes 36503552 | tf_op jit(solution)/shard_map/dot_general | solution.py:68
  162.5 15.2 %fusion.9 = f32[80,8192]{1,0:T(8,128)} fusion(bf16[2048,8192]{1,0:T(8,128)(2,1)} %param.10, bf16[336,2048]{1,0:T(8,128)(2,1)S(1)} %broadcast_select_fusion), kind=kOutput, calls=%fused_computation.42 | convolution fusion | flops 2684354560 | bytes 36503552 | tf_op jit(solution)/shard_map/dot_general | solution.py:68
  180.7 4.4 all-to-all-start.1
  185.2 15.1 %fusion.5 = f32[96,8192]{1,0:T(8,128)} fusion(bf16[2048,8192]{1,0:T(8,128)(2,1)} %param.10, bf16[336,2048]{1,0:T(8,128)(2,1)S(1)} %broadcast_select_fusion), kind=kOutput, calls=%fused_computation.38 | convolution fusion | flops 3221225472 | bytes 37093376 | tf_op jit(solution)/shard_map/dot_general | solution.py:68
  200.3 30.6 %reduce-scatter.10.cloned.1.call-done = f32[80,2048]{1,0:T(8,128)} async-done(((f32[80,8192]{1,0:T(8,128)}), f32[80,2048]{1,0:T(8,128)}) %reduce-scatter.10.cloned.1.call-update) | async-done | bytes 655376 | tf_op jit(solution)/shard_map/reduce_scatter | solution.py:69
  233.9 4.4 all-to-all-start.4
  238.2 46.6 %reduce-scatter.12.cloned.1.call-done = f32[80,2048]{1,0:T(8,128)} async-done(((f32[80,8192]{1,0:T(8,128)}), f32[80,2048]{1,0:T(8,128)}) %reduce-scatter.12.cloned.1.call-update) | async-done | bytes 655376 | tf_op jit(solution)/shard_map/reduce_scatter | solution.py:69
  287.9 4.4 all-to-all-start.5
  292.3 54.7 %reduce-scatter.14.cloned.1.call-done = f32[96,2048]{1,0:T(8,128)} async-done(((f32[96,8192]{1,0:T(8,128)}), f32[96,2048]{1,0:T(8,128)}) %reduce-scatter.14.cloned.1.call-update) | async-done | bytes 786448 | tf_op jit(solution)/shard_map/reduce_scatter | solution.py:69
  350.3 4.5 all-to-all-start.6
  354.9 37.6 %all-to-all-done.6 = bf16[8,96,2048]{2,1,0:T(8,128)(2,1)} async-done(((bf16[8,96,2048]{2,1,0:T(8,128)(2,1)}), bf16[8,96,2048]{2,1,0:T(8,128)(2,1)}, u32[]{:S(2)}, u32[]{:S(2)}) %all-to-all-start.6) | async-done | bytes 3145760 | tf_op jit(solution)/shard_map/all_to_all | solution.py:74
  392.6 10.6 %pad_maximum_fusion = bf16[8,336,2048]{2,1,0:T(8,128)(2,1)} fusion(bf16[8,96,2048]{2,1,0:T(8,128)(2,1)} %all-to-all-done.6, bf16[8,80,2048]{2,1,0:T(8,128)(2,1)} %all-to-all-done.5, bf16[8,80,2048]{2,1,0:T(8,128)(2,1)} %all-to-all-done.4, bf16[8,80,2048]{2,1,0:T(8,128)(2,1)} %all-to-all-done.1), kind=kLoop, calls=%fused_computation.34 | loop fusion | flops 44040192 | bytes 22020096 | tf_op jit(solution)/shard_map/concatenate | solution.py:76
  403.2 428.2 %while.14 = (s32[]{:T(128)}, f32[2048,256]{1,0:T(8,128)}, s32[16,8]{0,1:T(8,128)S(1)}, bf16[2688,2048]{1,0:T(8,128)(2,1)}, pred[16,8,32]{2,1,0:T(8,128)(4,1)S(1)...) while((s32[]{:T(128)}, f32[2048,256]{1,0:T(8,128)}, ...), condition=%wide.region_8.9_spmd.clone, body=%wide.region_7.8_spmd.clone.sunk | while | flops 270073888 | bytes 7735039 | solution.py:88
  478.7 3.5 fusion.38
  693.6 3.5 fusion.38
  (377 shorter events, 220.4 us)
Async XLA Ops:
  6.5 22.8 %copy-start = (bf16[512,2048]{1,0:T(8,128)(2,1)S(1)}, bf16[512,2048]{1,0:T(8,128)(2,1)}, u32[]{:S(2)}) copy-start(bf16[512,2048]{1,0:T(8,128)(2,1)} %param.11) | copy-start | bytes 6291460
  8.7 18.6 %all-to-all-start.2 = ((bf16[8,64,512]{2,1,0:T(8,128)(2,1)}), bf16[8,64,512]{2,1,0:T(8,128)(2,1)S(1)}, u32[]{:S(2)}, u32[]{:S(2)}) async-start(bf16[8,64,512]{2,1,0:T(8,128)(2,1)} %bitcast.22), calls=%async_computation.3 | async-start | bytes 1048576 | tf_op jit(solution)/shard_map/all_to_all | solution.py:15
  13.9 74.0 %reduce-scatter.8.cloned.1.call-start = ((), (), s32[]{:S(2)}) async-start(), calls=%async_computation.13 | async-start | bytes 3440640 | tf_op jit(solution)/shard_map/reduce_scatter | solution.py:45
  31.8 1.6 copy-start.2
  35.8 30.8 %all-to-all-start = ((bf16[8,64,2048]{2,1,0:T(8,128)(2,1)}), bf16[8,64,2048]{2,1,0:T(8,128)(2,1)S(1)}, u32[]{:S(2)}, u32[]{:S(2)}) async-start(bf16[8,64,2048]{2,1,0:T(8,128)(2,1)} %bitcast.71), calls=%async_computation | async-start | bytes 4194304 | tf_op jit(solution)/shard_map/all_to_all | solution.py:15
  40.0 83.3 %all-gather.2.cloned.1.call-start = ((), (), s32[]{:S(2)}) async-start(), calls=%async_computation.14 | async-start | bytes 1720320 | tf_op jit(solution)/shard_map/all_gather | solution.py:46
  89.8 87.9 %reduce-scatter.6.cloned.1.call-start = ((), (), s32[]{:S(2)}) async-start(), calls=%async_computation.12 | async-start | bytes 3276800 | tf_op jit(solution)/shard_map/reduce_scatter | solution.py:69
  105.5 125.4 %reduce-scatter.10.cloned.1.call-start = ((), (), s32[]{:S(2)}) async-start(), calls=%async_computation.15 | async-start | bytes 3276800 | tf_op jit(solution)/shard_map/reduce_scatter | solution.py:69
  162.2 122.7 %reduce-scatter.12.cloned.1.call-start = ((), (), s32[]{:S(2)}) async-start(), calls=%async_computation.16 | async-start | bytes 3276800 | tf_op jit(solution)/shard_map/reduce_scatter | solution.py:69
  180.7 51.3 %all-to-all-start.1 = ((bf16[8,80,2048]{2,1,0:T(8,128)(2,1)}), bf16[8,80,2048]{2,1,0:T(8,128)(2,1)}, u32[]{:S(2)}, u32[]{:S(2)}) async-start(bf16[8,80,2048]{2,1,0:T(8,128)(2,1)} %broadcast_in_dim.79), calls=%async_computation.2 | async-start | bytes 5242880 | tf_op jit(solution)/shard_map/all_to_all | solution.py:74
  185.2 161.9 %reduce-scatter.14.cloned.1.call-start = ((), (), s32[]{:S(2)}) async-start(), calls=%async_computation.17 | async-start | bytes 3932160 | tf_op jit(solution)/shard_map/reduce_scatter | solution.py:69
  233.9 52.2 %all-to-all-start.4 = ((bf16[8,80,2048]{2,1,0:T(8,128)(2,1)}), bf16[8,80,2048]{2,1,0:T(8,128)(2,1)}, u32[]{:S(2)}, u32[]{:S(2)}) async-start(bf16[8,80,2048]{2,1,0:T(8,128)(2,1)} %broadcast_in_dim.80), calls=%async_computation.7 | async-start | bytes 5242880 | tf_op jit(solution)/shard_map/all_to_all | solution.py:74
  287.9 60.3 %all-to-all-start.5 = ((bf16[8,80,2048]{2,1,0:T(8,128)(2,1)}), bf16[8,80,2048]{2,1,0:T(8,128)(2,1)}, u32[]{:S(2)}, u32[]{:S(2)}) async-start(bf16[8,80,2048]{2,1,0:T(8,128)(2,1)} %broadcast_in_dim.81), calls=%async_computation.9 | async-start | bytes 5242880 | tf_op jit(solution)/shard_map/all_to_all | solution.py:74
  350.3 42.3 %all-to-all-start.6 = ((bf16[8,96,2048]{2,1,0:T(8,128)(2,1)}), bf16[8,96,2048]{2,1,0:T(8,128)(2,1)}, u32[]{:S(2)}, u32[]{:S(2)}) async-start(bf16[8,96,2048]{2,1,0:T(8,128)(2,1)} %broadcast_in_dim.82), calls=%async_computation.11 | async-start | bytes 6291456 | tf_op jit(solution)/shard_map/all_to_all | solution.py:74
  831.4 3.2 copy-start.1
Sparse Core Ops, SparseCore 0:
  31.9 55.9 reduce-scatter.7
  89.9 33.2 all-gather.1
  125.6 51.2 reduce-scatter.5
  179.1 51.7 reduce-scatter.9
  233.0 51.7 reduce-scatter.11
  287.0 59.9 reduce-scatter.13
where the time goes:
time: 849 us; the launch traced here: 841 us
  loops' own time  237 us (28%)
  waiting for transfers between devices  233 us (27%)
  local copies, waits for them, and re-layouts  160 us (19%)
  matrix products  117 us (14%)
  other arithmetic  31.5 us (4%)
  starting transfers between devices  27.4 us (3%)
  blocking collectives  22.3 us (3%)
  between operations  13.7 us (2%)
    another operation x1, loops' own time, shards(): squares = lax.fori_loop(0, nseq, one_slot, squares)  237 us
    reduce_scatter x4, waiting for transfers between devices, shards(): lax.psum_scatter(grad_part, 'tensor', scatter_dimension=1, tiled=True)  132 us
    while x224, local copies, waits for them, and re-layouts  110 us
    dot_general x4, matrix products, shards(): grad_part = jnp.dot(block, basis_out, preferred_element_type=jnp.float32)  60.9 us
    dot_general x16, matrix products, one_slot(): lax.dot_general(g_s, a_s, (((0,), (0,)), ((), ())), preferred_element_typ...  53.7 us
    all_to_all x4, waiting for transfers between devices, shards(): got = lax.all_to_all(sent, 'dp', 0, 0, tiled=True)  37.7 us
    all_to_all x2, waiting for transfers between devices, redistribute(): return lax.all_to_all(x, 'dp', 0, 0, tiled=True)  26.6 us
    all_to_all x1, blocking collectives, shards(): rot_acts = lax.all_to_all(act_whole, 'dp', 0, 0, tiled=True)  22.3 us
  transfers between devices with their start and end apart: 12, of which 7 were waited for; matrix products, arithmetic and copies ran while one was open for 11% of the time, Pallas kernels for 0%

commit v1 on v0

--- a/solution.py
+++ b/solution.py
@@ -43,7 +43,16 @@
     acts_p = jnp.take(acts_r, src, axis=0, mode="clip")
     act_part = jnp.dot(acts_p, basis_in, preferred_element_type=jnp.float32)
     act_sum = lax.psum_scatter(act_part, "tensor", scatter_dimension=1, tiled=True)
-    act_whole = lax.all_gather(act_sum.astype(jnp.bfloat16), "tensor", axis=1, tiled=True)
+    shard = act_sum.astype(jnp.bfloat16)
+    ways, here, lap = (lax.axis_size("tensor"), lax.axis_index("tensor"), shard.shape[1])
+    line, have = (shard, 1)
+    while have < ways:
+        line = jnp.concatenate(
+            [line, lax.ppermute(line, "tensor", [(d, (d - have) % ways) for d in range(ways)])],
+            axis=1,
+        )
+        have = 2 * have
+    act_whole = jnp.roll(line, here * lap, axis=1)
     in_cols = act_whole.shape[1] // dp
     act_whole = act_whole.reshape(cap, dp, in_cols).transpose(1, 0, 2).reshape(-1, in_cols)
     rot_acts = lax.all_to_all(act_whole, "dp", 0, 0, tiled=True)

time: 849 us -> 881 us (1.038)
  waiting for transfers between devices: 233 us -> 258 us
    ppermute x0 -> x2, waiting for transfers between devices: none -> 76.5 us  [shards(): lax.ppermute(line, 'tensor', [(d, (d - have) % ways) for d in range(ways)])]
    reduce_scatter x4, waiting for transfers between devices: 132 us -> 111 us  [shards(): lax.psum_scatter(grad_part, 'tensor', scatter_dimension=1, tiled=True)]
    all_gather x1 -> x0, waiting for transfers between devices: 17.7 us -> none  [shards(): lax.all_gather(act_sum.astype(jnp.bfloat16), 'tensor', axis=1, tiled=True)]
    reduce_scatter x1, waiting for transfers between devices: 18.9 us -> 3.45 us  [shards(): lax.psum_scatter(act_part, 'tensor', scatter_dimension=1, tiled=True)]
  transfers between devices with their start and end apart: 12 -> 13, of which waited for: 7 -> 9; matrix products, arithmetic and copies ran while one was open for 11% -> 11% of each run, Pallas kernels for 0% -> 0%
where the time goes in v1:
time: 881 us; the launch traced here: 873 us
  waiting for transfers between devices  258 us (29%)
  loops' own time  237 us (27%)
  local copies, waits for them, and re-layouts  165 us (19%)
  matrix products  117 us (13%)
  other arithmetic  31.6 us (4%)
  starting transfers between devices  29.2 us (3%)
  blocking collectives  21.9 us (2%)
  between operations  13.4 us (2%)
    another operation x1, loops' own time, shards(): squares = lax.fori_loop(0, nseq, one_slot, squares)  237 us
    reduce_scatter x4, waiting for transfers between devices, shards(): lax.psum_scatter(grad_part, 'tensor', scatter_dimension=1, tiled=True)  111 us
    while x224, local copies, waits for them, and re-layouts  110 us
    ppermute x2, waiting for transfers between devices, shards(): lax.ppermute(line, 'tensor', [(d, (d - have) % ways) for d in range(ways)])  76.5 us
    dot_general x4, matrix products, shards(): grad_part = jnp.dot(block, basis_out, preferred_element_type=jnp.float32)  61 us
    dot_general x16, matrix products, one_slot(): lax.dot_general(g_s, a_s, (((0,), (0,)), ((), ())), preferred_element_typ...  53.8 us
    all_to_all x4, waiting for transfers between devices, shards(): got = lax.all_to_all(sent, 'dp', 0, 0, tiled=True)  40.7 us
    all_to_all x2, waiting for transfers between devices, redistribute(): return lax.all_to_all(x, 'dp', 0, 0, tiled=True)  26.6 us
  transfers between devices with their start and end apart: 13, of which 9 were waited for; matrix products, arithmetic and copies ran while one was open for 11% of the time, Pallas kernels for 0%

profile of v1, /device:TPU:0, one launch (start us, length us, event | category | flops | bytes accessed | tf_op | source)
XLA Modules:
  0.0 873.2 jit_solution(12375529929914311482)
XLA Ops:
  8.7 5.2 all-to-all-start.2
  17.2 4.3 fusion.22
  21.5 5.7 select_select_fusion
  35.8 4.1 all-to-all-start
  40.0 26.6 %all-to-all-done = bf16[8,64,2048]{2,1,0:T(8,128)(2,1)S(1)} async-done(((bf16[8,64,2048]{2,1,0:T(8,128)(2,1)}), bf16[8,64,2048]{2,1,0:T(8,128)(2,1)S(1)}, u32[]{:S(2)}, u32[]{:S(2)}) %all-to-all-start) | async-done | bytes 2097184 | tf_op jit(solution)/shard_map/all_to_all | solution.py:15
  69.2 15.2 %fusion.7 = f32[80,8192]{1,0:T(8,128)} fusion(bf16[2048,8192]{1,0:T(8,128)(2,1)} %param.10, bf16[336,2048]{1,0:T(8,128)(2,1)S(1)} %broadcast_select_fusion), kind=kOutput, calls=%fused_computation.40 | convolution fusion | flops 2684354560 | bytes 36503552 | tf_op jit(solution)/shard_map/dot_general | solution.py:77
  91.6 12.6 %collective-permute-done = bf16[336,512]{1,0:T(8,128)(2,1)S(1)} collective-permute-done((bf16[336,512]{1,0:T(8,128)(2,1)S(1)}, bf16[336,512]{1,0:T(8,128)(2,1)S(1)}, u32[]{:S(2)}, u32[]{:S(2)}) %collective-permute-start) | collective-permute-done | bytes 344096 | tf_op jit(solution)/shard_map/ppermute | solution.py:51
  105.2 63.9 %collective-permute-done.1 = bf16[336,1024]{1,0:T(8,128)(2,1)S(1)} collective-permute-done((bf16[336,1024]{1,0:T(8,128)(2,1)S(1)}, bf16[336,1024]{1,0:T(8,128)(2,1)S(1)}, u32[]{:S(2)}, u32[]{:S(2)}) %collective-permute-start.1) | collective-permute-done | bytes 688160 | tf_op jit(solution)/shard_map/ppermute | solution.py:51
  174.6 21.9 %all_to_all.57 = bf16[8,336,256]{2,1,0:T(8,128)(2,1)S(1)} all-to-all(bf16[8,336,256]{2,1,0:T(8,128)(2,1)S(1)} %copy.23), channel_id=1, replica_groups=mesh['dp'=8,'tensor'=4] {'dp'}, dimensions={0} | all-to-all | bytes 2752512 | tf_op jit(solution)/shard_map/all_to_all | solution.py:58
  196.6 15.1 %fusion.11 = f32[80,8192]{1,0:T(8,128)} fusion(bf16[2048,8192]{1,0:T(8,128)(2,1)} %param.10, bf16[336,2048]{1,0:T(8,128)(2,1)S(1)} %broadcast_select_fusion), kind=kOutput, calls=%fused_computation.44 | convolution fusion | flops 2684354560 | bytes 36503552 | tf_op jit(solution)/shard_map/dot_general | solution.py:77
  211.9 15.5 %fusion.9 = f32[80,8192]{1,0:T(8,128)} fusion(bf16[2048,8192]{1,0:T(8,128)(2,1)} %param.10, bf16[336,2048]{1,0:T(8,128)(2,1)S(1)} %broadcast_select_fusion), kind=kOutput, calls=%fused_computation.42 | convolution fusion | flops 2684354560 | bytes 36503552 | tf_op jit(solution)/shard_map/dot_general | solution.py:77
  230.5 4.4 all-to-all-start.1
  234.9 15.1 %fusion.5 = f32[96,8192]{1,0:T(8,128)} fusion(bf16[2048,8192]{1,0:T(8,128)(2,1)} %param.10, bf16[336,2048]{1,0:T(8,128)(2,1)S(1)} %broadcast_select_fusion), kind=kOutput, calls=%fused_computation.38 | convolution fusion | flops 3221225472 | bytes 37093376 | tf_op jit(solution)/shard_map/dot_general | solution.py:77
  250.1 12.9 %reduce-scatter.10.cloned.1.call-done = f32[80,2048]{1,0:T(8,128)} async-done(((f32[80,8192]{1,0:T(8,128)}), f32[80,2048]{1,0:T(8,128)}) %reduce-scatter.10.cloned.1.call-update) | async-done | bytes 655376 | tf_op jit(solution)/shard_map/reduce_scatter | solution.py:78
  269.0 4.4 all-to-all-start.4
  273.4 43.6 %reduce-scatter.12.cloned.1.call-done = f32[80,2048]{1,0:T(8,128)} async-done(((f32[80,8192]{1,0:T(8,128)}), f32[80,2048]{1,0:T(8,128)}) %reduce-scatter.12.cloned.1.call-update) | async-done | bytes 655376 | tf_op jit(solution)/shard_map/reduce_scatter | solution.py:78
  320.0 4.4 all-to-all-start.5
  324.4 54.7 %reduce-scatter.14.cloned.1.call-done = f32[96,2048]{1,0:T(8,128)} async-done(((f32[96,8192]{1,0:T(8,128)}), f32[96,2048]{1,0:T(8,128)}) %reduce-scatter.14.cloned.1.call-update) | async-done | bytes 786448 | tf_op jit(solution)/shard_map/reduce_scatter | solution.py:78
  382.4 4.5 all-to-all-start.6
  387.0 37.6 %all-to-all-done.6 = bf16[8,96,2048]{2,1,0:T(8,128)(2,1)} async-done(((bf16[8,96,2048]{2,1,0:T(8,128)(2,1)}), bf16[8,96,2048]{2,1,0:T(8,128)(2,1)}, u32[]{:S(2)}, u32[]{:S(2)}) %all-to-all-start.6) | async-done | bytes 3145760 | tf_op jit(solution)/shard_map/all_to_all | solution.py:83
  424.7 10.6 %pad_maximum_fusion = bf16[8,336,2048]{2,1,0:T(8,128)(2,1)} fusion(bf16[8,96,2048]{2,1,0:T(8,128)(2,1)} %all-to-all-done.6, bf16[8,80,2048]{2,1,0:T(8,128)(2,1)} %all-to-all-done.5, bf16[8,80,2048]{2,1,0:T(8,128)(2,1)} %all-to-all-done.4, bf16[8,80,2048]{2,1,0:T(8,128)(2,1)} %all-to-all-done.1), kind=kLoop, calls=%fused_computation.34 | loop fusion | flops 44040192 | bytes 22020096 | tf_op jit(solution)/shard_map/concatenate | solution.py:85
  435.3 428.2 %while.14 = (s32[]{:T(128)}, f32[2048,256]{1,0:T(8,128)}, s32[16,8]{0,1:T(8,128)S(1)}, bf16[2688,2048]{1,0:T(8,128)(2,1)}, pred[16,8,32]{2,1,0:T(8,128)(4,1)S(1)...) while((s32[]{:T(128)}, f32[2048,256]{1,0:T(8,128)}, ...), condition=%wide.region_8.9_spmd.clone, body=%wide.region_7.8_spmd.clone.sunk | while | flops 270073888 | bytes 7735039 | solution.py:97
  537.7 3.5 fusion.38
  591.4 3.5 fusion.38
  (386 shorter events, 233.8 us)
Async XLA Ops:
  6.5 22.8 %copy-start = (bf16[512,2048]{1,0:T(8,128)(2,1)S(1)}, bf16[512,2048]{1,0:T(8,128)(2,1)}, u32[]{:S(2)}) copy-start(bf16[512,2048]{1,0:T(8,128)(2,1)} %param.11) | copy-start | bytes 6291460
  8.7 18.6 %all-to-all-start.2 = ((bf16[8,64,512]{2,1,0:T(8,128)(2,1)}), bf16[8,64,512]{2,1,0:T(8,128)(2,1)S(1)}, u32[]{:S(2)}, u32[]{:S(2)}) async-start(bf16[8,64,512]{2,1,0:T(8,128)(2,1)} %bitcast.22), calls=%async_computation.3 | async-start | bytes 1048576 | tf_op jit(solution)/shard_map/all_to_all | solution.py:15
  13.9 74.0 %reduce-scatter.8.cloned.1.call-start = ((), (), s32[]{:S(2)}) async-start(), calls=%async_computation.13 | async-start | bytes 3440640 | tf_op jit(solution)/shard_map/reduce_scatter | solution.py:45
  31.8 1.6 copy-start.2
  35.8 30.8 %all-to-all-start = ((bf16[8,64,2048]{2,1,0:T(8,128)(2,1)}), bf16[8,64,2048]{2,1,0:T(8,128)(2,1)S(1)}, u32[]{:S(2)}, u32[]{:S(2)}) async-start(bf16[8,64,2048]{2,1,0:T(8,128)(2,1)} %bitcast.68), calls=%async_computation | async-start | bytes 4194304 | tf_op jit(solution)/shard_map/all_to_all | solution.py:15
  40.0 187.5 %reduce-scatter.6.cloned.1.call-start = ((), (), s32[]{:S(2)}) async-start(), calls=%async_computation.12 | async-start | bytes 3276800 | tf_op jit(solution)/shard_map/reduce_scatter | solution.py:78
  84.4 178.5 %reduce-scatter.10.cloned.1.call-start = ((), (), s32[]{:S(2)}) async-start(), calls=%async_computation.14 | async-start | bytes 3276800 | tf_op jit(solution)/shard_map/reduce_scatter | solution.py:78
  89.9 14.3 %collective-permute-start = (bf16[336,512]{1,0:T(8,128)(2,1)S(1)}, bf16[336,512]{1,0:T(8,128)(2,1)S(1)}, u32[]{:S(2)}, u32[]{:S(2)}) collective-permute-start(bf16[336,512]{1,0:T(8,128)(2,1)S(1)} %get-tuple-element.195), channel_id=1, source_target_pairs={{0,3},{1,0},{2,1},{3,2},{4,7},{5,4},{6,5},{7,6},{8,11},{9,8},{10,9... | collective-permute-start | bytes 1032200 | tf_op jit(solution)/shard_map/ppermute | solution.py:51
  104.3 64.8 %collective-permute-start.1 = (bf16[336,1024]{1,0:T(8,128)(2,1)S(1)}, bf16[336,1024]{1,0:T(8,128)(2,1)S(1)}, u32[]{:S(2)}, u32[]{:S(2)}) collective-permute-start(bf16[336,1024]{1,0:T(8,128)(2,1)S(1)} %pad_maximum_fusion.1), channel_id=1, source_target_pairs={{0,2},{1,3},{2,0},{3,1},{4,6},{5,7},{6,4},{7,5},{8,10},{9,11},{10,... | collective-permute-start | bytes 2064392 | tf_op jit(solution)/shard_map/ppermute | solution.py:51
  211.7 105.3 %reduce-scatter.12.cloned.1.call-start = ((), (), s32[]{:S(2)}) async-start(), calls=%async_computation.15 | async-start | bytes 3276800 | tf_op jit(solution)/shard_map/reduce_scatter | solution.py:78
  230.5 36.7 %all-to-all-start.1 = ((bf16[8,80,2048]{2,1,0:T(8,128)(2,1)}), bf16[8,80,2048]{2,1,0:T(8,128)(2,1)}, u32[]{:S(2)}, u32[]{:S(2)}) async-start(bf16[8,80,2048]{2,1,0:T(8,128)(2,1)} %broadcast_in_dim.79), calls=%async_computation.2 | async-start | bytes 5242880 | tf_op jit(solution)/shard_map/all_to_all | solution.py:83
  234.9 144.2 %reduce-scatter.14.cloned.1.call-start = ((), (), s32[]{:S(2)}) async-start(), calls=%async_computation.16 | async-start | bytes 3932160 | tf_op jit(solution)/shard_map/reduce_scatter | solution.py:78
  269.0 49.1 %all-to-all-start.4 = ((bf16[8,80,2048]{2,1,0:T(8,128)(2,1)}), bf16[8,80,2048]{2,1,0:T(8,128)(2,1)}, u32[]{:S(2)}, u32[]{:S(2)}) async-start(bf16[8,80,2048]{2,1,0:T(8,128)(2,1)} %broadcast_in_dim.80), calls=%async_computation.7 | async-start | bytes 5242880 | tf_op jit(solution)/shard_map/all_to_all | solution.py:83
  320.0 60.3 %all-to-all-start.5 = ((bf16[8,80,2048]{2,1,0:T(8,128)(2,1)}), bf16[8,80,2048]{2,1,0:T(8,128)(2,1)}, u32[]{:S(2)}, u32[]{:S(2)}) async-start(bf16[8,80,2048]{2,1,0:T(8,128)(2,1)} %broadcast_in_dim.81), calls=%async_computation.9 | async-start | bytes 5242880 | tf_op jit(solution)/shard_map/all_to_all | solution.py:83
  382.4 42.3 %all-to-all-start.6 = ((bf16[8,96,2048]{2,1,0:T(8,128)(2,1)}), bf16[8,96,2048]{2,1,0:T(8,128)(2,1)}, u32[]{:S(2)}, u32[]{:S(2)}) async-start(bf16[8,96,2048]{2,1,0:T(8,128)(2,1)} %broadcast_in_dim.82), calls=%async_computation.11 | async-start | bytes 6291456 | tf_op jit(solution)/shard_map/all_to_all | solution.py:83
  863.5 3.2 copy-start.1
Sparse Core Ops, SparseCore 0:
  31.9 55.9 reduce-scatter.7
  90.2 76.9 reduce-scatter.5
  211.8 51.1 reduce-scatter.9
  265.1 51.8 reduce-scatter.11
  319.1 59.9 reduce-scatter.13
